TPU v7x, 128 devices: a whole 4x4x4 slice. The times are simulated.
128 devices in a mesh: req: 16 (over y, z), mlp: 8 (over x, core).
Axes of the slice: x: 4, y: 4, z: 4, core: 2. Of those that a mesh axis runs over, the one named last changes fastest.
Arguments:
- tokens: bfloat16 [32768, 1536], P(('req', 'mlp')), may hold values from -6 to 6
- attn_gain: float32 [1536], replicated, may hold values from 0.1 to 1.9
- w_query: bfloat16 [1536, 1536], replicated, may hold values from -0.15625 to 0.15625
- w_keyval: bfloat16 [1536, 256], replicated, may hold values from -0.15625 to 0.15625
- w_out: bfloat16 [1536, 1536], replicated, may hold values from -0.15625 to 0.15625
- ffn_gain: float32 [1536], replicated, may hold values from 0.1 to 1.9
- w_gate: bfloat16 [1536, 4608], P('req', 'mlp'), may hold values from -0.15625 to 0.15625
- w_up: bfloat16 [1536, 4608], P('req', 'mlp'), may hold values from -0.15625 to 0.15625
- w_down: bfloat16 [1536, 4608], P('req', 'mlp'), may hold values from -0.09375 to 0.09375
- prefix_kv: bfloat16 [2, 128, 512, 256], P(None, 'req'), may hold values from -60 to 60, as said below
- own_prefix: bfloat16 [16, 512, 256], P('req'), may hold values from -60 to 60, as said below
- leaf_parent: int32 [16], replicated, may hold values from 0 to 127
- node_parent: int32 [128], replicated, may hold values from 0 to 127
- seg_lengths: int32 [3, 128], replicated, may hold values from 1 to 512
Outputs:
- layer_out: bfloat16 [32768, 1536], P(('req', 'mlp'))
Inputs may be any that keep to these rules, and one draw needn't show every extreme that they name: `prefix_kv`: columns below 128 are keys, the rest values. `own_prefix`: columns below 128 are keys, the rest values.
All inputs are finite; a program needn't handle non-finite values.
Results may differ from a plain program's by a relative error of at most 0.018.
Values may be sent and summed in bfloat16 or wider, within the bound.
No kernel may reach another device: no remote copies, remote signals or barrier semaphores. Data moves between devices by JAX's collectives and lax.ppermute only.
A program may use at most 192 MiB of HBM per device.

v0:
```python
import jax
import jax.numpy as jnp
from jax import lax
from jax.sharding import PartitionSpec as P

HEADS = 12
HD = 128
WINDOW = 1024
EPS = 1e-06


def rms_scale(values, gain):
    wide = values.astype(jnp.float32)
    return wide * lax.rsqrt(jnp.mean(wide * wide, axis=-1, keepdims=True) + EPS) * gain


def rotate(values, where_at):
    half_dim = values.shape[-1] // 2
    freqs = 10000.0 ** (-jnp.arange(half_dim, dtype=jnp.float32) / half_dim)
    angles = where_at.astype(jnp.float32)[:, None] * freqs[None, :]
    cosine = jnp.cos(angles)[:, None, :]
    sine = jnp.sin(angles)[:, None, :]
    first = values[..., :half_dim]
    second = values[..., half_dim:]
    return jnp.concatenate([first * cosine - second * sine, first * sine + second * cosine], -1)


def attend(queries, piece, key_at, key_live, query_at):
    scores = jnp.einsum("thd,kd->thk", queries, piece[:, :HD], preferred_element_type=jnp.float32)
    spacing = query_at[:, None] - key_at[None, :]
    allowed = (key_live[None, :] & (spacing >= 0) & (spacing < WINDOW))[:, None, :]
    top = jnp.max(jnp.where(allowed, scores, -jnp.inf), axis=-1)
    safe_top = jnp.where(jnp.isfinite(top), top, 0.0)
    weights = jnp.where(allowed, jnp.exp(scores - safe_top[..., None]), 0.0)
    mixed = jnp.einsum(
        "thk,kd->thd",
        weights.astype(jnp.bfloat16),
        piece[:, HD:],
        preferred_element_type=jnp.float32,
    )
    return (top, jnp.sum(weights, axis=-1), mixed)


def combine(first, second):
    top = jnp.maximum(first[0], second[0])
    safe_top = jnp.where(jnp.isfinite(top), top, 0.0)
    scale_first = jnp.exp(first[0] - safe_top)
    scale_second = jnp.exp(second[0] - safe_top)
    denom = first[1] * scale_first + second[1] * scale_second
    mixed = first[2] * scale_first[..., None] + second[2] * scale_second[..., None]
    return (top, denom, mixed)


def body(
    tokens,
    attn_gain,
    w_query,
    w_keyval,
    w_out,
    ffn_gain,
    w_gate,
    w_up,
    w_down,
    prefix_kv,
    own_prefix,
    leaf_parent,
    node_parent,
    seg_lengths,
):
    tok_rows = tokens.shape[0]
    requests = lax.axis_size("req")
    mine = lax.axis_index("req")
    position_group = lax.axis_index("mlp")
    node_dev = prefix_kv.shape[1]
    seg_slot = prefix_kv.shape[2]
    leaf = leaf_parent[mine]
    upper = node_parent[leaf]
    len_zero = seg_lengths[0, upper]
    len_one = seg_lengths[1, leaf]
    len_two = seg_lengths[2, mine]
    total = len_zero + len_one + len_two
    query_at = total + position_group * tok_rows + jnp.arange(tok_rows, dtype=jnp.int32)
    normed = rms_scale(tokens, attn_gain).astype(jnp.bfloat16)
    query_full = jnp.dot(normed, w_query, preferred_element_type=jnp.float32).reshape(
        tok_rows, HEADS, HD
    )
    queries = (rotate(query_full, query_at) * HD ** (-0.5)).astype(jnp.bfloat16)
    keyval_full = jnp.dot(normed, w_keyval, preferred_element_type=jnp.float32)
    new_keys = rotate(keyval_full[:, None, :HD], query_at)[:, 0].astype(jnp.bfloat16)
    new_vals = keyval_full[:, HD:].astype(jnp.bfloat16)
    new_keyval = jnp.concatenate([new_keys, new_vals], 1)
    start_state = (
        jnp.full((tok_rows, HEADS), -jnp.inf, jnp.float32),
        jnp.zeros((tok_rows, HEADS), jnp.float32),
        jnp.zeros((tok_rows, HEADS, HD), jnp.float32),
    )
    piece = lax.all_gather(new_keyval, "mlp", axis=0, tiled=True)
    piece_at = total + jnp.arange(piece.shape[0], dtype=jnp.int32)
    live = jnp.ones((piece.shape[0],), dtype=bool)
    own_state = combine(start_state, attend(queries, piece, piece_at, live, query_at))
    level_zero = node_parent[leaf_parent]
    wanted = jnp.stack([level_zero, leaf_parent], 1)
    owned = wanted // node_dev == mine
    local_slot = wanted % node_dev
    picker = (
        (local_slot[:, :, None] == jnp.arange(node_dev, dtype=jnp.int32)[None, None, :])
        & owned[:, :, None]
    ).astype(jnp.bfloat16)
    owners = wanted[mine] // node_dev
    from_owner = (jnp.arange(requests, dtype=jnp.int32)[:, None] == owners[None, :]).astype(
        jnp.bfloat16
    )
    outgoing = jnp.einsum(
        "rln,lnsc->rlsc", picker, prefix_kv, preferred_element_type=jnp.float32
    ).astype(jnp.bfloat16)
    arrived = lax.all_to_all(outgoing, "req", split_axis=0, concat_axis=0, tiled=True)
    levels = jnp.einsum(
        "rl,rlsc->lsc", from_owner, arrived, preferred_element_type=jnp.float32
    ).astype(jnp.bfloat16)
    offsets = jnp.arange(seg_slot, dtype=jnp.int32)
    cached = jnp.concatenate([levels[0], levels[1], own_prefix[0]], 0)
    cached_at = jnp.concatenate([offsets, len_zero + offsets, len_zero + len_one + offsets], 0)
    cached_live = jnp.concatenate([offsets < len_zero, offsets < len_one, offsets < len_two], 0)
    merged = combine(own_state, attend(queries, cached, cached_at, cached_live, query_at))
    context = (merged[2] / merged[1][..., None]).reshape(tok_rows, HEADS * HD).astype(jnp.bfloat16)
    attn_out = jnp.dot(context, w_out, preferred_element_type=jnp.float32)
    resid = (tokens.astype(jnp.float32) + attn_out).astype(jnp.bfloat16)
    ffn_in = rms_scale(resid, ffn_gain).astype(jnp.bfloat16)
    all_rows = lax.all_gather(ffn_in, "mlp", axis=0, tiled=True)
    gate_full, up_full, down_full = (
        lax.all_gather(w_gate, "req", axis=0, tiled=True),
        lax.all_gather(w_up, "req", axis=0, tiled=True),
        lax.all_gather(w_down, "req", axis=0, tiled=True),
    )
    gate = jnp.dot(all_rows, gate_full, preferred_element_type=jnp.float32)
    upward = jnp.dot(all_rows, up_full, preferred_element_type=jnp.float32)
    hidden = (jax.nn.gelu(gate, approximate=True) * upward).astype(jnp.bfloat16)
    summed = lax.psum_scatter(
        lax.dot_general(
            hidden, down_full, (((1,), (1,)), ((), ())), preferred_element_type=jnp.float32
        ).astype(jnp.bfloat16),
        "mlp",
        scatter_dimension=0,
        tiled=True,
    ).astype(jnp.float32)
    return (resid.astype(jnp.float32) + summed).astype(jnp.bfloat16)


def solution(mesh):
    return jax.shard_map(
        body,
        mesh=mesh,
        in_specs=(
            P(("req", "mlp"), None),
            P(),
            P(),
            P(),
            P(),
            P(),
            P("req", "mlp"),
            P("req", "mlp"),
            P("req", "mlp"),
            P(None, "req", None, None),
            P("req", None, None),
            P(),
            P(),
            P(),
        ),
        out_specs=P(("req", "mlp"), None),
        check_vma=False,
    )
```

profile of v0, /device:TPU:1, one launch (start us, length us, event | category | flops | bytes accessed | tf_op | source)
XLA Modules:
  0.0 438.2 jit_solution(3613787128685627271)
XLA Ops:
  6.6 1.3 dynamic_slice.18
  9.8 1.2 dynamic_slice.19
  12.4 1.4 fusion.25
  13.8 1.7 fusion.35
  16.1 1.5 constant_dynamic-slice_fusion
  19.5 0.3 fusion.44
  19.8 0.7 pad_maximum_fusion.1
  20.5 0.0 all-gather.6.cloned.1.call-update
  20.5 0.7 compare_select_fusion
  21.2 0.7 gather_fusion
  21.9 7.2 %convert_bitcast_fusion = bf16[16,2,512,256]{3,0,2,1:T(8,128)(2,1)} fusion(bf16[2,8,512,256]{3,2,1,0:T(8,128)(2,1)} %param.23, s32[16,2]{0,1:T(2,128)S(1)} %get-tuple-element.24, pred[16,2]{0,1:T(4,128)(4,1)S(1)} %fusion.54), kind=kOutput, calls=%fused_computation.15 | convolution fusion | flops 71303680 | bytes 12583072 | tf_op jit(solution)/shard_map/rln,lnsc->rlsc/dot_general | solution.py:113
  29.1 9.6 %copy.33 = bf16[16,2,512,256]{3,2,1,0:T(8,128)(2,1)} copy(bf16[16,2,512,256]{3,0,2,1:T(8,128)(2,1)} %convert_bitcast_fusion) | data formatting | bytes 16777216 | tf_op jit(solution)/shard_map/convert_element_type | solution.py:115
  38.8 8.9 %all-to-all-start = ((bf16[16,2,512,256]{3,2,1,0:T(8,128)(2,1)}), bf16[16,2,512,256]{3,2,1,0:T(8,128)(2,1)}, u32[]{:S(2)}, u32[]{:S(2)}) async-start(bf16[16,2,512,256]{3,2,1,0:T(8,128)(2,1)} %copy.33), calls=%async_computation | async-start | bytes 16777216 | tf_op jit(solution)/shard_map/all_to_all | solution.py:116
  47.7 0.0 all-gather.10.cloned.1.call-start
  47.7 0.7 all-gather.10.cloned.1.call-update
  48.4 0.3 all-gather.8.cloned.1.call-start
  48.8 0.0 copy-done.3
  48.8 0.0 copy-done.9
  48.8 4.3 fusion.37
  53.1 0.1 fusion.62
  53.3 0.5 copy.45
  53.8 1.6 copy.44
  55.4 0.2 fusion.53
  55.6 0.1 copy.38
  55.7 0.6 iota_compare_fusion.4
  56.4 1.3 iota_compare_fusion.2
  57.6 0.6 iota_add_fusion.1
  58.3 0.5 multiply_cosine_fusion
  58.8 1.9 multiply_subtract_fusion
  60.7 0.5 fusion.28
  61.2 0.5 fusion.24
  61.7 0.5 fusion.30
  62.3 0.0 all-gather.6.cloned.1.call-done
  62.3 11.8 %select_reduce_fusion = (f32[256,12]{0,1:T(8,128)S(1)}, f32[256,12,2048]{2,0,1:T(8,128)}) fusion(pred[256,2048]{1,0:T(8,128)(4,1)S(1)} %fusion.24, bf16[256,12,128]{2,0,1:T(8,128)(2,1)S(1)} %fusion.28, bf16[2048,256]{0,1:T(8,128)(2,1)} %all-gather.6.cloned.1.call-done), kind=kOutput, calls=%fused_computation.2 | convolution fusion | flops 1623192576 | bytes 27013120 | tf_op jit(solution)/shard_map/thd,kd->thk/dot_general | solution.py:29
  74.2 11.3 %fusion = f32[256,12]{0,1:T(8,128)S(1)} fusion(f32[256,12,2048]{2,0,1:T(8,128)} %get-tuple-element.27, f32[256,12]{0,1:T(8,128)S(1)} %get-tuple-element.18, pred[256,2048]{1,0:T(8,128)(4,1)S(1)} %fusion.24), kind=kLoop, calls=%fused_computation.3 | loop fusion | flops 18871296 | bytes 25714688 | tf_op jit(solution)/shard_map/reduce_sum | solution.py:41
  85.5 11.8 %fusion.4 = f32[256,12,128]{0,2,1:T(8,128)} fusion(f32[256,12,2048]{2,0,1:T(8,128)} %get-tuple-element.27, f32[256,12]{0,1:T(8,128)S(1)} %get-tuple-element.18, pred[256,2048]{1,0:T(8,128)(4,1)S(1)} %fusion.24, bf16[2048,256]{0,1:T(8,128)(2,1)S(1)} %copy-done.5), kind=kOutput, calls=%fused_computation.9 | convolution fusion | flops 1629487104 | bytes 27803648 | tf_op jit(solution)/shard_map/thk,kd->thd/dot_general | solution.py:35
  97.3 97.6 %all-to-all-done = bf16[16,2,512,256]{3,2,1,0:T(8,128)(2,1)} async-done(((bf16[16,2,512,256]{3,2,1,0:T(8,128)(2,1)}), bf16[16,2,512,256]{3,2,1,0:T(8,128)(2,1)}, u32[]{:S(2)}, u32[]{:S(2)}) %all-to-all-start) | async-done | bytes 8388640 | tf_op jit(solution)/shard_map/all_to_all | solution.py:116
  194.9 8.3 %fusion.10 = bf16[2,1,512,256]{3,1,2,0:T(2,128)(2,1)S(1)} fusion(pred[16,2,1,1]{0,2,3,1:T(4,128)(4,1)S(1)} %copy.38, bf16[16,2,512,256]{3,2,1,0:T(8,128)(2,1)} %all-to-all-done), kind=kOutput, calls=%fused_computation.13 | convolution fusion | flops 8388608 | bytes 8912928 | tf_op jit(solution)/shard_map/rl,rlsc->lsc/dot_general | solution.py:117
  203.2 0.1 copy.51
  203.3 0.1 pad_maximum_fusion
  203.4 8.0 %select_reduce_fusion.1 = (f32[256,12]{0,1:T(8,128)S(1)}, f32[256,12,1536]{2,0,1:T(8,128)}) fusion(pred[256,1536]{1,0:T(8,128)(4,1)S(1)} %fusion.30, bf16[256,12,128]{2,0,1:T(8,128)(2,1)S(1)} %fusion.28, bf16[1536,256]{1,0:T(8,128)(2,1)S(1)} %pad_maximum_fusion), kind=kOutput, calls=%fused_computation.6 | convolution fusion | flops 1217393664 | bytes 20459520 | tf_op jit(solution)/shard_map/thd,kd->thk/dot_general | solution.py:29
  211.5 0.0 slice-start
  211.5 10.5 %fusion.2 = f32[256,12]{0,1:T(8,128)S(1)} fusion(f32[256,12,1536]{2,0,1:T(8,128)} %get-tuple-element.29, f32[256,12]{0,1:T(8,128)S(1)} %is-finite_select_fusion, pred[256,1536]{1,0:T(8,128)(4,1)S(1)} %fusion.30), kind=kLoop, calls=%fused_computation.7 | loop fusion | flops 14152704 | bytes 19292160 | tf_op jit(solution)/shard_map/reduce_sum | solution.py:41
  222.0 0.0 slice-start.1
  222.0 0.0 copy-start.4
  222.0 8.7 %divide_convert_fusion = bf16[256,12,128]{0,2,1:T(8,128)(2,1)S(1)} fusion(f32[256,12,128]{0,2,1:T(8,128)} %fusion.4, f32[256,12,1536]{2,0,1:T(8,128)} %get-tuple-element.29, f32[256,12]{0,1:T(8,128)S(1)} %is-finite_select_fusion, pred[256,1536]{1,0:T(8,128)(4,1)S(1)} %fusion.30, f32[256,12]{0,1:T(8,128)S(1)} %get-tuple-element.5, ...), kind=kOutput, calls=%fused_computation.46 | convolution fusion | flops 1224867840 | bytes 22118400 | tf_op jit(solution)/shard_map/thk,kd->thd/dot_general | solution.py:35
  230.8 0.0 copy-start.7
  230.8 1.5 multiply_reduce_fusion
  232.3 1.1 multiply_convert_fusion
  233.4 0.0 all-gather.8.cloned.1.call-update
  233.4 0.0 all-gather.14.cloned.1.call-start
  233.5 0.5 all-gather.14.cloned.1.call-update
  234.0 0.0 all-gather.12.cloned.1.call-start
  234.1 0.5 all-gather.12.cloned.1.call-update
  234.6 0.0 reduce-scatter.2.cloned.1.call-start
  234.7 0.0 all-gather.10.cloned.1.call-done
  234.7 44.8 %all-gather.8.cloned.1.call-done = bf16[2048,1536]{1,0:T(8,128)(2,1)} async-done(((bf16[256,1536]{1,0:T(8,128)(2,1)}), bf16[2048,1536]{1,0:T(8,128)(2,1)}) %all-gather.8.cloned.1.call-update) | async-done | bytes 6291472 | tf_op jit(solution)/shard_map/all_gather | solution.py:129
  279.4 9.3 %fusion.63 = f32[2048,576]{0,1:T(8,128)} fusion(bf16[2048,1536]{1,0:T(8,128)(2,1)} %all-gather.8.cloned.1.call-done, bf16[1536,576]{1,0:T(8,128)(2,1)} %all-gather.10.cloned.1.call-done), kind=kOutput, calls=%fused_computation.133 | convolution fusion | flops 3623878656 | bytes 12779520 | tf_op jit(solution)/shard_map/dot_general | solution.py:135
  288.8 36.4 %all-gather.14.cloned.1.call-done = bf16[1536,576]{1,0:T(8,128)(2,1)} async-done(((bf16[96,576]{1,0:T(8,128)(2,1)}), bf16[1536,576]{1,0:T(8,128)(2,1)}) %all-gather.14.cloned.1.call-update) | async-done | bytes 1769488 | tf_op jit(solution)/shard_map/all_gather | solution.py:133
  325.2 46.1 %all-gather.12.cloned.1.call-done = bf16[1536,576]{1,0:T(8,128)(2,1)} async-done(((bf16[96,576]{1,0:T(8,128)(2,1)}), bf16[1536,576]{1,0:T(8,128)(2,1)}) %all-gather.12.cloned.1.call-update) | async-done | bytes 1769488 | tf_op jit(solution)/shard_map/all_gather | solution.py:132
  371.2 15.6 %convolution_convert_fusion = bf16[2048,1536]{1,0:T(8,128)(2,1)} fusion(bf16[1536,576]{1,0:T(8,128)(2,1)} %all-gather.14.cloned.1.call-done, f32[2048,576]{0,1:T(8,128)} %fusion.63, bf16[2048,1536]{1,0:T(8,128)(2,1)} %all-gather.8.cloned.1.call-done, bf16[1536,576]{1,0:T(8,128)(2,1)} %all-gather.12.cloned.1.call-done), kind=kOutput, calls=%fused_computation.16 | convolution fusion | flops 7262699520 | bytes 20840448 | tf_op jit(solution)/shard_map/dot_general | solution.py:139
  386.8 0.0 reduce-scatter.2.cloned.1.call-update
  386.8 42.0 %reduce-scatter.2.cloned.1.call-done = bf16[256,1536]{1,0:T(8,128)(2,1)} async-done(((bf16[2048,1536]{1,0:T(8,128)(2,1)}), bf16[256,1536]{1,0:T(8,128)(2,1)}) %reduce-scatter.2.cloned.1.call-update) | async-done | bytes 786448 | tf_op jit(solution)/shard_map/reduce_scatter | solution.py:138
  428.9 2.2 add_convert_fusion
  (40 shorter events, 0.3 us)
Async XLA Ops:
  6.5 7.2 %copy-start = (bf16[1536,256]{1,0:T(8,128)(2,1)S(1)}, bf16[1536,256]{1,0:T(8,128)(2,1)}, u32[]{:S(2)}) copy-start(bf16[1536,256]{1,0:T(8,128)(2,1)} %param.17) | copy-start | bytes 2359300
  6.5 15.3 %copy-start.8 = (s32[16]{0:T(128)S(1)}, s32[16]{0:T(128)}, u32[]{:S(2)}) copy-start(s32[16]{0:T(128)} %param.25) | copy-start | bytes 196
  6.5 14.7 %copy-start.2 = (s32[128]{0:T(128)S(1)}, s32[128]{0:T(128)}, u32[]{:S(2)}) copy-start(s32[128]{0:T(128)} %param.26) | copy-start | bytes 1540
  6.5 55.8 %all-gather.6.cloned.1.call-start = ((), (), s32[]{:S(2)}) async-start(), calls=%async_computation.2 | async-start | bytes 1179648 | tf_op jit(solution)/shard_map/all_gather | solution.py:97
  38.8 10.0 %copy-start.3 = (bf16[256,1536]{1,0:T(8,128)(2,1)S(1)}, bf16[256,1536]{1,0:T(8,128)(2,1)}, u32[]{:S(2)}) copy-start(bf16[256,1536]{1,0:T(8,128)(2,1)} %param.14) | copy-start | bytes 2359300
  38.8 10.0 %copy-start.9 = (f32[1536]{0:T(1024)S(1)}, f32[1536]{0:T(1024)}, u32[]{:S(2)}) copy-start(f32[1536]{0:T(1024)} %param.15) | copy-start | bytes 18436
  38.8 156.1 %all-to-all-start = ((bf16[16,2,512,256]{3,2,1,0:T(8,128)(2,1)}), bf16[16,2,512,256]{3,2,1,0:T(8,128)(2,1)}, u32[]{:S(2)}, u32[]{:S(2)}) async-start(bf16[16,2,512,256]{3,2,1,0:T(8,128)(2,1)} %copy.33), calls=%async_computation | async-start | bytes 16777216 | tf_op jit(solution)/shard_map/all_to_all | solution.py:116
  47.7 187.0 %all-gather.10.cloned.1.call-start = ((), (), s32[]{:S(2)}) async-start(), calls=%async_computation.4 | async-start | bytes 2088960 | tf_op jit(solution)/shard_map/all_gather | solution.py:131
  48.4 231.0 %all-gather.8.cloned.1.call-start = ((), (), s32[]{:S(2)}) async-start(), calls=%async_computation.3 | async-start | bytes 7077888 | tf_op jit(solution)/shard_map/all_gather | solution.py:129
  74.2 11.4 %copy-start.5 = (bf16[2048,256]{0,1:T(8,128)(2,1)S(1)}, bf16[2048,256]{0,1:T(8,128)(2,1)}, u32[]{:S(2)}) copy-start(bf16[2048,256]{0,1:T(8,128)(2,1)} %all-gather.6.cloned.1.call-done) | copy-start | bytes 3145732
  97.3 106.0 %copy-start.6 = (bf16[1,512,256]{2,1,0:T(8,128)(2,1)S(1)}, bf16[1,512,256]{2,1,0:T(8,128)(2,1)}, u32[]{:S(2)}) copy-start(bf16[1,512,256]{2,1,0:T(8,128)(2,1)} %param.24) | copy-start | bytes 786436
  211.5 19.3 %slice-start = ((s8[4718592]{0:T(1024)(128)(4,1)}), s8[524288]{0:T(1024)(128)(4,1)S(1)}, s32[]{:S(2)}) async-start(s8[4718592]{0:T(1024)(128)(4,1)} %bitcast.58), calls=%async_computation.8 | async-start | bytes 1048576
  222.0 8.8 %slice-start.1 = ((s8[4718592]{0:T(1024)(128)(4,1)}), s8[4194304]{0:T(1024)(128)(4,1)S(1)}, s32[]{:S(2)}) async-start(s8[4718592]{0:T(1024)(128)(4,1)} %bitcast.58), calls=%async_computation.9 | async-start | bytes 8388608
  222.0 8.8 %copy-start.4 = (bf16[256,1536]{1,0:T(8,128)(2,1)S(1)}, bf16[256,1536]{1,0:T(8,128)(2,1)}, u32[]{:S(2)}) copy-start(bf16[256,1536]{1,0:T(8,128)(2,1)} %param.14) | copy-start | bytes 2359300
  230.8 1.5 copy-start.7
  233.4 91.7 %all-gather.14.cloned.1.call-start = ((), (), s32[]{:S(2)}) async-start(), calls=%async_computation.6 | async-start | bytes 2088960 | tf_op jit(solution)/shard_map/all_gather | solution.py:133
  234.0 137.2 %all-gather.12.cloned.1.call-start = ((), (), s32[]{:S(2)}) async-start(), calls=%async_computation.5 | async-start | bytes 2088960 | tf_op jit(solution)/shard_map/all_gather | solution.py:132
  234.6 194.3 %reduce-scatter.2.cloned.1.call-start = ((), (), s32[]{:S(2)}) async-start(), calls=%async_computation.7 | async-start | bytes 7077888 | tf_op jit(solution)/shard_map/reduce_scatter | solution.py:138
  386.8 44.3 %copy-start.1 = (bf16[1536,256]{1,0:T(8,128)(2,1)S(1)}, bf16[1536,256]{1,0:T(8,128)(2,1)}, u32[]{:S(2)}) copy-start(bf16[1536,256]{1,0:T(8,128)(2,1)} %param.17) | copy-start | bytes 2359300
Sparse Core Ops, SparseCore 0:
  20.7 26.9 all-gather.5
  50.7 139.0 all-gather.9
  233.6 45.8 all-gather.7
  281.5 43.6 all-gather.13
  327.2 43.9 all-gather.11
  387.0 41.8 reduce-scatter.1
where the time goes:
time: 444 us; the launch traced here: 438 us
  waiting for transfers between devices  269 us (61%)
  matrix products  88.4 us (20%)
  other arithmetic  35 us (8%)
  between operations  19.9 us (4%)
  local copies, waits for them, and re-layouts  16.9 us (4%)
  starting transfers between devices  9.38 us (2%)
    all_to_all x1, waiting for transfers between devices, body(): lax.all_to_all(outgoing, 'req', split_axis=0, concat_axis=0, tiled=True)  97.6 us
    all_gather x1, waiting for transfers between devices, body(): lax.all_gather(w_up, 'req', axis=0, tiled=True)  46.1 us
    all_gather x1, waiting for transfers between devices, body(): all_rows = lax.all_gather(ffn_in, 'mlp', axis=0, tiled=True)  44.8 us
    reduce_scatter x1, waiting for transfers between devices, body(): lax.psum_scatter(lax.dot_general(hidden, down_full, (((1,), (1,)), ((), (...  42 us
    all_gather x1, waiting for transfers between devices, body(): lax.all_gather(w_down, 'req', axis=0, tiled=True)  36.4 us
    reduce_sum x2, other arithmetic, attend(): return (top, jnp.sum(weights, axis=-1), mixed)  21.8 us
    dot_general x2, matrix products, attend(): jnp.einsum('thk,kd->thd', weights.astype(jnp.bfloat16), piece[:, HD:], pr...  20.5 us
    dot_general x2, matrix products, attend(): jnp.einsum('thd,kd->thk', queries, piece[:, :HD], preferred_element_type=...  19.9 us
  transfers between devices with their start and end apart: 7, of which 5 were waited for; matrix products, arithmetic and copies ran while one was open for 26% of the time, Pallas kernels for 0%

commit v1 on v0

--- a/solution.py
+++ b/solution.py
@@ -127,9 +127,13 @@
     resid = (tokens.astype(jnp.float32) + attn_out).astype(jnp.bfloat16)
     ffn_in = rms_scale(resid, ffn_gain).astype(jnp.bfloat16)
     all_rows = lax.all_gather(ffn_in, "mlp", axis=0, tiled=True)
+    edit_paths = lambda xs, mesh_name: jnp.concatenate(
+        lax.all_to_all(jnp.stack([xs for _ in range(lax.axis_size(mesh_name))]), mesh_name, 0, 0),
+        axis=0,
+    )
     gate_full, up_full, down_full = (
         lax.all_gather(w_gate, "req", axis=0, tiled=True),
-        lax.all_gather(w_up, "req", axis=0, tiled=True),
+        edit_paths(w_up, "req"),
         lax.all_gather(w_down, "req", axis=0, tiled=True),
     )
     gate = jnp.dot(all_rows, gate_full, preferred_element_type=jnp.float32)

time: 444 us -> 398 us (0.90)
  waiting for transfers between devices: 269 us -> 213 us
  starting transfers between devices: 9.38 us -> 17.8 us
    all_gather x1 -> x0, waiting for transfers between devices: 46.1 us -> none  [body(): lax.all_gather(w_up, 'req', axis=0, tiled=True)]
    all_gather x1, waiting for transfers between devices: 44.8 us -> 35.4 us  [body(): all_rows = lax.all_gather(ffn_in, 'mlp', axis=0, tiled=True)]
    all_to_all x0 -> x1, starting transfers between devices: none -> 8.5 us  [body(): lax.all_to_all(jnp.stack([xs for _ in range(lax.axis_size(mesh_name))]),...]
  transfers between devices with their start and end apart: 7 -> 7, of which waited for: 5 -> 4; matrix products, arithmetic and copies ran while one was open for 26% -> 30% of each run, Pallas kernels for 0% -> 0%
where the time goes in v1:
time: 398 us; the launch traced here: 392 us
  waiting for transfers between devices  213 us (54%)
  matrix products  88.3 us (22%)
  other arithmetic  35 us (9%)
  between operations  19.6 us (5%)
  local copies, waits for them, and re-layouts  18.4 us (5%)
  starting transfers between devices  17.8 us (4%)
    all_to_all x1, waiting for transfers between devices, body(): lax.all_to_all(outgoing, 'req', split_axis=0, concat_axis=0, tiled=True)  97.6 us
    reduce_scatter x1, waiting for transfers between devices, body(): lax.psum_scatter(lax.dot_general(hidden, down_full, (((1,), (1,)), ((), (...  42.1 us
    all_gather x1, waiting for transfers between devices, body(): lax.all_gather(w_down, 'req', axis=0, tiled=True)  36.4 us
    all_gather x1, waiting for transfers between devices, body(): all_rows = lax.all_gather(ffn_in, 'mlp', axis=0, tiled=True)  35.4 us
    reduce_sum x2, other arithmetic, attend(): return (top, jnp.sum(weights, axis=-1), mixed)  21.8 us
    dot_general x2, matrix products, attend(): jnp.einsum('thk,kd->thd', weights.astype(jnp.bfloat16), piece[:, HD:], pr...  20.5 us
    dot_general x2, matrix products, attend(): jnp.einsum('thd,kd->thk', queries, piece[:, :HD], preferred_element_type=...  19.9 us
    dot_general x1, matrix products, body(): lax.dot_general(hidden, down_full, (((1,), (1,)), ((), ())), preferred_el...  15.6 us
  transfers between devices with their start and end apart: 7, of which 4 were waited for; matrix products, arithmetic and copies ran while one was open for 30% of the time, Pallas kernels for 0%

profile of v1, /device:TPU:1, one launch (start us, length us, event | category | flops | bytes accessed | tf_op | source)
XLA Modules:
  0.0 391.8 jit_solution(3532366713728168644)
XLA Ops:
  6.6 1.3 dynamic_slice.18
  9.8 1.2 dynamic_slice.19
  12.4 1.4 fusion.25
  13.8 1.7 fusion.35
  16.1 1.5 constant_dynamic-slice_fusion
  19.5 0.3 fusion.44
  19.8 0.7 pad_maximum_fusion.1
  20.5 0.0 all-gather.5.cloned.1.call-update
  20.5 0.7 compare_select_fusion
  21.2 0.7 gather_fusion
  21.9 7.2 %convert_bitcast_fusion = bf16[16,2,512,256]{3,0,2,1:T(8,128)(2,1)} fusion(bf16[2,8,512,256]{3,2,1,0:T(8,128)(2,1)} %param.23, s32[16,2]{0,1:T(2,128)S(1)} %get-tuple-element.24, pred[16,2]{0,1:T(4,128)(4,1)S(1)} %fusion.54), kind=kOutput, calls=%fused_computation.15 | convolution fusion | flops 71303680 | bytes 12583072 | tf_op jit(solution)/shard_map/rln,lnsc->rlsc/dot_general | solution.py:113
  29.1 9.6 %copy.33 = bf16[16,2,512,256]{3,2,1,0:T(8,128)(2,1)} copy(bf16[16,2,512,256]{3,0,2,1:T(8,128)(2,1)} %convert_bitcast_fusion) | data formatting | bytes 16777216 | tf_op jit(solution)/shard_map/convert_element_type | solution.py:115
  38.8 8.9 %all-to-all-start = ((bf16[16,2,512,256]{3,2,1,0:T(8,128)(2,1)}), bf16[16,2,512,256]{3,2,1,0:T(8,128)(2,1)}, u32[]{:S(2)}, u32[]{:S(2)}) async-start(bf16[16,2,512,256]{3,2,1,0:T(8,128)(2,1)} %copy.33), calls=%async_computation | async-start | bytes 16777216 | tf_op jit(solution)/shard_map/all_to_all | solution.py:116
  47.7 0.0 all-gather.9.cloned.1.call-start
  47.7 0.7 all-gather.9.cloned.1.call-update
  48.4 0.3 all-gather.7.cloned.1.call-start
  48.8 0.0 copy-done.3
  48.8 4.3 %fusion.37 = f32[256,1536]{0,1:T(8,128)S(1)} fusion(bf16[1536,1536]{1,0:T(8,128)(2,1)} %param.16, bf16[256,1536]{1,0:T(8,128)(2,1)S(1)} %copy-done.3, f32[1536]{0:T(1024)S(1)} %copy-done.10, f32[256]{0:T(256)S(1)} %add_rsqrt_fusion.1), kind=kOutput, calls=%fused_computation.62 | convolution fusion | flops 1209532416 | bytes 7085056 | tf_op jit(solution)/shard_map/dot_general | solution.py:84
  53.1 0.1 fusion.62
  53.3 0.5 copy.45
  53.8 1.6 copy.44
  55.4 0.2 fusion.53
  55.6 0.1 copy.38
  55.7 0.6 iota_compare_fusion.4
  56.4 1.3 iota_compare_fusion.2
  57.6 0.6 iota_add_fusion.1
  58.3 0.5 multiply_cosine_fusion
  58.8 1.9 multiply_subtract_fusion
  60.7 0.5 fusion.28
  61.2 0.5 fusion.24
  61.7 0.5 fusion.30
  62.3 0.0 all-gather.5.cloned.1.call-done
  62.3 11.8 %select_reduce_fusion = (f32[256,12]{0,1:T(8,128)S(1)}, f32[256,12,2048]{2,0,1:T(8,128)}) fusion(pred[256,2048]{1,0:T(8,128)(4,1)S(1)} %fusion.24, bf16[256,12,128]{2,0,1:T(8,128)(2,1)S(1)} %fusion.28, bf16[2048,256]{0,1:T(8,128)(2,1)} %all-gather.5.cloned.1.call-done), kind=kOutput, calls=%fused_computation.2 | convolution fusion | flops 1623192576 | bytes 27013120 | tf_op jit(solution)/shard_map/thd,kd->thk/dot_general | solution.py:29
  74.2 11.3 %fusion = f32[256,12]{0,1:T(8,128)S(1)} fusion(f32[256,12,2048]{2,0,1:T(8,128)} %get-tuple-element.27, f32[256,12]{0,1:T(8,128)S(1)} %get-tuple-element.18, pred[256,2048]{1,0:T(8,128)(4,1)S(1)} %fusion.24), kind=kLoop, calls=%fused_computation.3 | loop fusion | flops 18871296 | bytes 25714688 | tf_op jit(solution)/shard_map/reduce_sum | solution.py:41
  85.5 11.8 %fusion.4 = f32[256,12,128]{0,2,1:T(8,128)} fusion(f32[256,12,2048]{2,0,1:T(8,128)} %get-tuple-element.27, f32[256,12]{0,1:T(8,128)S(1)} %get-tuple-element.18, pred[256,2048]{1,0:T(8,128)(4,1)S(1)} %fusion.24, bf16[2048,256]{0,1:T(8,128)(2,1)S(1)} %copy-done.5), kind=kOutput, calls=%fused_computation.9 | convolution fusion | flops 1629487104 | bytes 27803648 | tf_op jit(solution)/shard_map/thk,kd->thd/dot_general | solution.py:35
  97.3 97.6 %all-to-all-done = bf16[16,2,512,256]{3,2,1,0:T(8,128)(2,1)} async-done(((bf16[16,2,512,256]{3,2,1,0:T(8,128)(2,1)}), bf16[16,2,512,256]{3,2,1,0:T(8,128)(2,1)}, u32[]{:S(2)}, u32[]{:S(2)}) %all-to-all-start) | async-done | bytes 8388640 | tf_op jit(solution)/shard_map/all_to_all | solution.py:116
  194.9 8.3 %fusion.10 = bf16[2,1,512,256]{3,1,2,0:T(2,128)(2,1)S(1)} fusion(pred[16,2,1,1]{0,2,3,1:T(4,128)(4,1)S(1)} %copy.38, bf16[16,2,512,256]{3,2,1,0:T(8,128)(2,1)} %all-to-all-done), kind=kOutput, calls=%fused_computation.13 | convolution fusion | flops 8388608 | bytes 8912928 | tf_op jit(solution)/shard_map/rl,rlsc->lsc/dot_general | solution.py:117
  203.2 0.1 copy.51
  203.3 0.1 pad_maximum_fusion
  203.4 8.0 %select_reduce_fusion.1 = (f32[256,12]{0,1:T(8,128)S(1)}, f32[256,12,1536]{2,0,1:T(8,128)}) fusion(pred[256,1536]{1,0:T(8,128)(4,1)S(1)} %fusion.30, bf16[256,12,128]{2,0,1:T(8,128)(2,1)S(1)} %fusion.28, bf16[1536,256]{1,0:T(8,128)(2,1)S(1)} %pad_maximum_fusion), kind=kOutput, calls=%fused_computation.6 | convolution fusion | flops 1217393664 | bytes 20459520 | tf_op jit(solution)/shard_map/thd,kd->thk/dot_general | solution.py:29
  211.5 0.0 slice-start
  211.5 10.5 %fusion.2 = f32[256,12]{0,1:T(8,128)S(1)} fusion(f32[256,12,1536]{2,0,1:T(8,128)} %get-tuple-element.29, f32[256,12]{0,1:T(8,128)S(1)} %is-finite_select_fusion, pred[256,1536]{1,0:T(8,128)(4,1)S(1)} %fusion.30), kind=kLoop, calls=%fused_computation.7 | loop fusion | flops 14152704 | bytes 19292160 | tf_op jit(solution)/shard_map/reduce_sum | solution.py:41
  222.0 0.0 slice-start.1
  222.0 0.0 copy-start.4
  222.0 8.7 %divide_convert_fusion = bf16[256,12,128]{0,2,1:T(8,128)(2,1)S(1)} fusion(f32[256,12,128]{0,2,1:T(8,128)} %fusion.4, f32[256,12,1536]{2,0,1:T(8,128)} %get-tuple-element.29, f32[256,12]{0,1:T(8,128)S(1)} %is-finite_select_fusion, pred[256,1536]{1,0:T(8,128)(4,1)S(1)} %fusion.30, f32[256,12]{0,1:T(8,128)S(1)} %get-tuple-element.5, ...), kind=kOutput, calls=%fused_computation.46 | convolution fusion | flops 1224867840 | bytes 22118400 | tf_op jit(solution)/shard_map/thk,kd->thd/dot_general | solution.py:35
  230.8 0.0 copy-start.8
  230.8 0.0 copy-start.7
  230.8 1.5 multiply_reduce_fusion
  232.3 1.1 multiply_convert_fusion
  233.4 0.0 all-gather.7.cloned.1.call-update
  233.5 0.0 all-gather.11.cloned.1.call-start
  233.5 0.5 all-gather.11.cloned.1.call-update
  234.0 1.5 stack.11
  235.5 8.5 %all-to-all-start.1 = ((bf16[16,96,576]{2,1,0:T(8,128)(2,1)}), bf16[16,96,576]{2,1,0:T(8,128)(2,1)}, u32[]{:S(2)}, u32[]{:S(2)}) async-start(bf16[16,96,576]{2,1,0:T(8,128)(2,1)} %stack.11), calls=%async_computation.1 | async-start | bytes 3932160 | tf_op jit(solution)/shard_map/all_to_all | solution.py:131
  244.0 0.0 reduce-scatter.2.cloned.1.call-start
  244.1 0.0 all-gather.9.cloned.1.call-done
  244.1 35.4 %all-gather.7.cloned.1.call-done = bf16[2048,1536]{1,0:T(8,128)(2,1)} async-done(((bf16[256,1536]{1,0:T(8,128)(2,1)}), bf16[2048,1536]{1,0:T(8,128)(2,1)}) %all-gather.7.cloned.1.call-update) | async-done | bytes 6291472 | tf_op jit(solution)/shard_map/all_gather | solution.py:129
  279.4 9.3 %fusion.63 = f32[2048,576]{0,1:T(8,128)} fusion(bf16[2048,1536]{1,0:T(8,128)(2,1)} %all-gather.7.cloned.1.call-done, bf16[1536,576]{1,0:T(8,128)(2,1)} %all-gather.9.cloned.1.call-done), kind=kOutput, calls=%fused_computation.133 | convolution fusion | flops 3623878656 | bytes 12779520 | tf_op jit(solution)/shard_map/dot_general | solution.py:139
  288.8 0.0 all-to-all-done.1
  288.8 36.4 %all-gather.11.cloned.1.call-done = bf16[1536,576]{1,0:T(8,128)(2,1)} async-done(((bf16[96,576]{1,0:T(8,128)(2,1)}), bf16[1536,576]{1,0:T(8,128)(2,1)}) %all-gather.11.cloned.1.call-update) | async-done | bytes 1769488 | tf_op jit(solution)/shard_map/all_gather | solution.py:137
  325.2 15.6 %convolution_convert_fusion = bf16[2048,1536]{1,0:T(8,128)(2,1)} fusion(bf16[1536,576]{1,0:T(8,128)(2,1)} %all-gather.11.cloned.1.call-done, f32[2048,576]{0,1:T(8,128)} %fusion.63, bf16[2048,1536]{1,0:T(8,128)(2,1)} %all-gather.7.cloned.1.call-done, bf16[1536,576]{1,0:T(8,128)(2,1)} %bitcast.23), kind=kOutput, calls=%fused_computation.16 | convolution fusion | flops 7262699520 | bytes 20840448 | tf_op jit(solution)/shard_map/dot_general | solution.py:143
  340.8 0.0 reduce-scatter.2.cloned.1.call-update
  340.8 42.1 %reduce-scatter.2.cloned.1.call-done = bf16[256,1536]{1,0:T(8,128)(2,1)} async-done(((bf16[2048,1536]{1,0:T(8,128)(2,1)}), bf16[256,1536]{1,0:T(8,128)(2,1)}) %reduce-scatter.2.cloned.1.call-update) | async-done | bytes 786448 | tf_op jit(solution)/shard_map/reduce_scatter | solution.py:142
  382.9 2.2 add_convert_fusion
  (42 shorter events, 0.3 us)
Async XLA Ops:
  6.5 7.2 %copy-start = (bf16[1536,256]{1,0:T(8,128)(2,1)S(1)}, bf16[1536,256]{1,0:T(8,128)(2,1)}, u32[]{:S(2)}) copy-start(bf16[1536,256]{1,0:T(8,128)(2,1)} %param.17) | copy-start | bytes 2359300
  6.5 15.3 %copy-start.9 = (s32[16]{0:T(128)S(1)}, s32[16]{0:T(128)}, u32[]{:S(2)}) copy-start(s32[16]{0:T(128)} %param.25) | copy-start | bytes 196
  6.5 14.7 %copy-start.2 = (s32[128]{0:T(128)S(1)}, s32[128]{0:T(128)}, u32[]{:S(2)}) copy-start(s32[128]{0:T(128)} %param.26) | copy-start | bytes 1540
  6.5 55.8 %all-gather.5.cloned.1.call-start = ((), (), s32[]{:S(2)}) async-start(), calls=%async_computation.3 | async-start | bytes 1179648 | tf_op jit(solution)/shard_map/all_gather | solution.py:97
  38.8 10.0 %copy-start.3 = (bf16[256,1536]{1,0:T(8,128)(2,1)S(1)}, bf16[256,1536]{1,0:T(8,128)(2,1)}, u32[]{:S(2)}) copy-start(bf16[256,1536]{1,0:T(8,128)(2,1)} %param.14) | copy-start | bytes 2359300
  38.8 10.0 %copy-start.10 = (f32[1536]{0:T(1024)S(1)}, f32[1536]{0:T(1024)}, u32[]{:S(2)}) copy-start(f32[1536]{0:T(1024)} %param.15) | copy-start | bytes 18436
  38.8 156.1 %all-to-all-start = ((bf16[16,2,512,256]{3,2,1,0:T(8,128)(2,1)}), bf16[16,2,512,256]{3,2,1,0:T(8,128)(2,1)}, u32[]{:S(2)}, u32[]{:S(2)}) async-start(bf16[16,2,512,256]{3,2,1,0:T(8,128)(2,1)} %copy.33), calls=%async_computation | async-start | bytes 16777216 | tf_op jit(solution)/shard_map/all_to_all | solution.py:116
  47.7 196.4 %all-gather.9.cloned.1.call-start = ((), (), s32[]{:S(2)}) async-start(), calls=%async_computation.5 | async-start | bytes 2088960 | tf_op jit(solution)/shard_map/all_gather | solution.py:135
  48.4 231.0 %all-gather.7.cloned.1.call-start = ((), (), s32[]{:S(2)}) async-start(), calls=%async_computation.4 | async-start | bytes 7077888 | tf_op jit(solution)/shard_map/all_gather | solution.py:129
  74.2 11.4 %copy-start.5 = (bf16[2048,256]{0,1:T(8,128)(2,1)S(1)}, bf16[2048,256]{0,1:T(8,128)(2,1)}, u32[]{:S(2)}) copy-start(bf16[2048,256]{0,1:T(8,128)(2,1)} %all-gather.5.cloned.1.call-done) | copy-start | bytes 3145732
  97.3 106.0 %copy-start.6 = (bf16[1,512,256]{2,1,0:T(8,128)(2,1)S(1)}, bf16[1,512,256]{2,1,0:T(8,128)(2,1)}, u32[]{:S(2)}) copy-start(bf16[1,512,256]{2,1,0:T(8,128)(2,1)} %param.24) | copy-start | bytes 786436
  211.5 19.3 %slice-start = ((s8[4718592]{0:T(1024)(128)(4,1)}), s8[524288]{0:T(1024)(128)(4,1)S(1)}, s32[]{:S(2)}) async-start(s8[4718592]{0:T(1024)(128)(4,1)} %bitcast.59), calls=%async_computation.8 | async-start | bytes 1048576
  222.0 8.8 %slice-start.1 = ((s8[4718592]{0:T(1024)(128)(4,1)}), s8[4194304]{0:T(1024)(128)(4,1)S(1)}, s32[]{:S(2)}) async-start(s8[4718592]{0:T(1024)(128)(4,1)} %bitcast.59), calls=%async_computation.9 | async-start | bytes 8388608
  222.0 8.8 %copy-start.4 = (bf16[256,1536]{1,0:T(8,128)(2,1)S(1)}, bf16[256,1536]{1,0:T(8,128)(2,1)}, u32[]{:S(2)}) copy-start(bf16[256,1536]{1,0:T(8,128)(2,1)} %param.14) | copy-start | bytes 2359300
  230.8 1.5 copy-start.8
  230.8 3.2 copy-start.7
  233.5 91.7 %all-gather.11.cloned.1.call-start = ((), (), s32[]{:S(2)}) async-start(), calls=%async_computation.6 | async-start | bytes 2088960 | tf_op jit(solution)/shard_map/all_gather | solution.py:137
  235.5 53.3 %all-to-all-start.1 = ((bf16[16,96,576]{2,1,0:T(8,128)(2,1)}), bf16[16,96,576]{2,1,0:T(8,128)(2,1)}, u32[]{:S(2)}, u32[]{:S(2)}) async-start(bf16[16,96,576]{2,1,0:T(8,128)(2,1)} %stack.11), calls=%async_computation.1 | async-start | bytes 3932160 | tf_op jit(solution)/shard_map/all_to_all | solution.py:131
  244.0 138.8 %reduce-scatter.2.cloned.1.call-start = ((), (), s32[]{:S(2)}) async-start(), calls=%async_computation.7 | async-start | bytes 7077888 | tf_op jit(solution)/shard_map/reduce_scatter | solution.py:142
  340.8 44.3 %copy-start.1 = (bf16[1536,256]{1,0:T(8,128)(2,1)S(1)}, bf16[1536,256]{1,0:T(8,128)(2,1)}, u32[]{:S(2)}) copy-start(bf16[1536,256]{1,0:T(8,128)(2,1)} %param.17) | copy-start | bytes 2359300
Sparse Core Ops, SparseCore 0:
  20.7 26.9 all-gather.4
  50.7 139.0 all-gather.8
  233.6 45.8 all-gather.6
  281.5 43.6 all-gather.10
  340.9 41.9 reduce-scatter.1
